TPU v7x, 32 devices: a whole 2x2x4 slice. The times are simulated.
32 devices in a mesh: axial: 8 (over y, x, core), radial: 4 (over z).
Axes of the slice: x: 2, y: 2, z: 4, core: 2. Of those that a mesh axis runs over, the one named last changes fastest.
Arguments:
- composition_deviations: float32 [38, 1024, 512], P(None, 'axial', 'radial'), may hold values from -6 to 6
- flow_speed_vector: float32 [2, 1024, 512], P(None, 'axial', 'radial'), may hold values from -1 to 1
- thermal_field: float32 [1024, 512], P('axial', 'radial'), may hold values from 0.4 to 4
- linearized_kinetics_operator: float32 [38, 38], replicated, may hold values from -0.5 to 0.5
- frozen_jacobian_inverse_addend: float32 [38, 38], replicated, may hold values from -0.25 to 0.25
- rigid_block_indicator: int32 [512, 4], P('axial', 'radial'), may hold values from 0 to 1, as said below
- molar_absorptivity_table: float32 [4, 38], replicated, may hold values from -1 to 1
- spokewise_sightline_length: float32 [512], P('radial'), may hold values from 0.3 to 3
- sightline_lengthwise_index: int32 [4, 32768], replicated, may hold values from 0 to 1023
- observed_absorbance_traces: float32 [4, 32768], P(None, ('axial', 'radial')), may hold values from -6 to 6
Outputs:
- species_out: float32 [38, 1024, 512], P(None, 'axial', 'radial')
- misfit: float32 [4, 32768], P(None, ('axial', 'radial'))
Inputs may be any that keep to these rules, and one draw needn't show every extreme that they name: `rigid_block_indicator`: in each radial column of tiles, the tiles of 2 cyclically consecutive axial devices are all stiff and every other axial device holds exactly 8 stiff tiles, so the column holds 176 stiff tiles.
All inputs are finite; a program needn't handle non-finite values.
Results may differ from a plain program's by a relative error of at most 0.0001.
Values sent between devices are 32-bit elements; how exact they have to be, the bound alone decides.
No kernel may reach another device: no remote copies, remote signals or barrier semaphores. Data moves between devices by JAX's collectives and lax.ppermute only.
A program may use at most 192 MiB of HBM per device.

v0:
```python
import math
import jax
import jax.numpy as jnp
from jax import lax
from jax.sharding import PartitionSpec as P

TILE_ROWS = 2
ITERS = 3
TIME_STEP = 0.4
CHEM_STEP = 0.5
ARRHENIUS_BARRIER = 1.0
WENO_EPS = 1e-06
HIGHEST = lax.Precision.HIGHEST


def extended(shard, sides, width):
    for axis, dim in sides:
        peers, length = (lax.axis_size(axis), shard.shape[dim])
        up = [(i, (i + 1) % peers) for i in range(peers - 1)]
        down = [(j, i) for i, j in up]
        last = lax.slice_in_dim(shard, length - width, length, axis=dim)
        initial = lax.slice_in_dim(shard, 0, width, axis=dim)
        before = lax.ppermute(last, axis, up)
        after = lax.ppermute(initial, axis, down)
        shard = jnp.concatenate([before, shard, after], axis=dim)
    return shard


def weno_side(minus_two, minus_one, centre, plus_one, plus_two):
    beta_zero = (
        13.0 / 12.0 * (minus_two - 2.0 * minus_one + centre) ** 2
        + 0.25 * (minus_two - 4.0 * minus_one + 3.0 * centre) ** 2
    )
    beta_one = (
        13.0 / 12.0 * (minus_one - 2.0 * centre + plus_one) ** 2
        + 0.25 * (minus_one - plus_one) ** 2
    )
    beta_two = (
        13.0 / 12.0 * (centre - 2.0 * plus_one + plus_two) ** 2
        + 0.25 * (3.0 * centre - 4.0 * plus_one + plus_two) ** 2
    )
    weight_zero = 0.1 / (WENO_EPS + beta_zero) ** 2
    weight_one = 0.6 / (WENO_EPS + beta_one) ** 2
    weight_two = 0.3 / (WENO_EPS + beta_two) ** 2
    weight_total = weight_zero + weight_one + weight_two
    blended = weight_zero * (2.0 * minus_two - 7.0 * minus_one + 11.0 * centre)
    blended = blended + weight_one * (-minus_one + 5.0 * centre + 2.0 * plus_one)
    blended = blended + weight_two * (2.0 * centre + 5.0 * plus_one - plus_two)
    return blended / (6.0 * weight_total)


def face_difference(field, speed, along, length):
    face_count = length + 1

    def cut_part(offset):
        return lax.slice_in_dim(field, offset, offset + face_count, axis=along)

    left_value = weno_side(cut_part(0), cut_part(1), cut_part(2), cut_part(3), cut_part(4))
    right_value = weno_side(cut_part(5), cut_part(4), cut_part(3), cut_part(2), cut_part(1))
    face_speed = 0.5 * (
        lax.slice_in_dim(speed, 2, 2 + face_count, axis=along)
        + lax.slice_in_dim(speed, 3, 3 + face_count, axis=along)
    )
    face_flux = (
        jnp.maximum(face_speed, 0.0) * left_value + jnp.minimum(face_speed, 0.0) * right_value
    )
    return lax.slice_in_dim(face_flux, 1, face_count, axis=along) - lax.slice_in_dim(
        face_flux, 0, face_count - 1, axis=along
    )


def transport(field_pad, speed_pad):
    row_count = field_pad.shape[1] - 6
    col_count = field_pad.shape[2] - 6
    along_axial = face_difference(field_pad[:, :, 3:-3], speed_pad[0:1, :, 3:-3], 1, row_count)
    along_radial = face_difference(field_pad[:, 3:-3, :], speed_pad[1:2, 3:-3, :], 2, col_count)
    return field_pad[:, 3:-3, 3:-3] - TIME_STEP * (along_axial + along_radial)


def kinetics_advance(
    starting_composition_field,
    thermal_field,
    linearized_kinetics_operator,
    frozen_jacobian_inverse_addend,
):
    acceleration_factor = jnp.exp(-ARRHENIUS_BARRIER / thermal_field)
    current = starting_composition_field
    for newton_step in range(ITERS):
        source = jnp.tensordot(
            linearized_kinetics_operator, current, axes=(1, 0), precision=HIGHEST
        ) - jnp.tanh(current)
        defect = current - starting_composition_field - CHEM_STEP * acceleration_factor * source
        current = (
            current
            - defect
            - jnp.tensordot(frozen_jacobian_inverse_addend, defect, axes=(1, 0), precision=HIGHEST)
        )
    return current


def absorbance_profile(field, molar_absorptivity_table, spokewise_sightline_length):
    mixed = jnp.tensordot(molar_absorptivity_table, field, axes=(1, 0), precision=HIGHEST)
    return jnp.dot(mixed, spokewise_sightline_length, precision=HIGHEST)


def local(
    composition_deviations,
    flow_speed_vector,
    thermal_field,
    linearized_kinetics_operator,
    frozen_jacobian_inverse_addend,
    rigid_block_indicator,
    molar_absorptivity_table,
    spokewise_sightline_length,
    sightline_lengthwise_index,
    observed_absorbance_traces,
):
    species_count = composition_deviations.shape[0]
    stacked = jnp.concatenate([composition_deviations, flow_speed_vector], axis=0)
    padded = extended(stacked, (("axial", 1), ("radial", 2)), 3)
    advected_composition_field = transport(padded[:species_count], padded[species_count:])
    combusted_composition_field = kinetics_advance(
        advected_composition_field,
        thermal_field,
        linearized_kinetics_operator,
        frozen_jacobian_inverse_addend,
    )
    flag_cells = jnp.repeat(
        jnp.repeat(rigid_block_indicator, TILE_ROWS, axis=0),
        advected_composition_field.shape[2],
        axis=1,
    )
    species_out = jnp.where(
        flag_cells[None] > 0, combusted_composition_field, advected_composition_field
    )
    path_scale = 1.0 / math.sqrt(advected_composition_field.shape[2] * lax.axis_size("radial"))
    profile = (
        absorbance_profile(species_out, molar_absorptivity_table, spokewise_sightline_length)
        * path_scale
    )
    column = lax.psum(profile, "radial")
    whole_profile = lax.all_gather(column, "axial", axis=1, tiled=True)
    device = lax.axis_index(("axial", "radial"))
    sample_count = observed_absorbance_traces.shape[1]
    own_rows = lax.dynamic_slice_in_dim(
        sightline_lengthwise_index, device * sample_count, sample_count, 1
    )
    values = jnp.take_along_axis(whole_profile, own_rows, axis=1)
    return (species_out, values - observed_absorbance_traces)


def solution(mesh):
    in_specs = (
        P(None, "axial", "radial"),
        P(None, "axial", "radial"),
        P("axial", "radial"),
        P(),
        P(),
        P("axial", "radial"),
        P(),
        P("radial"),
        P(),
        P(None, ("axial", "radial")),
    )
    out_specs = (P(None, "axial", "radial"), P(None, ("axial", "radial")))
    return jax.shard_map(local, mesh=mesh, in_specs=in_specs, out_specs=out_specs, check_vma=False)
```

profile of v0, /device:TPU:0, one launch (start us, length us, event | category | flops | bytes accessed | tf_op | source)
XLA Modules:
  0.0 168.7 jit_solution(240044641915545838)
XLA Ops:
  0.7 2.6 %copy.75 = f32[38,128,128]{1,0,2:T(8,128)S(1)} copy(f32[38,128,128]{2,1,0:T(8,128)} %param.10) | data formatting | bytes 4980736 | tf_op args[0]
  3.4 3.3 %slice_maximum_fusion = (f32[40,3,128]{1,0,2:T(8,128)}, f32[40,3,128]{1,0,2:T(8,128)}) fusion(f32[2,128,128]{1,0,2:T(2,128)S(1)} %copy.64, f32[38,128,128]{1,0,2:T(8,128)S(1)} %copy.75), kind=kLoop, calls=%fused_computation.63 | loop fusion | flops 30720 | bytes 2744320 | tf_op jit(solution)/shard_map/concatenate | solution.py:119
  6.7 2.5 %copy.67 = f32[40,3,128]{2,0,1:T(8,128)S(1)} copy(f32[40,3,128]{1,0,2:T(8,128)} %get-tuple-element.25) | data formatting | bytes 122880 | tf_op jit(solution)/shard_map/slice | solution.py:22
  10.5 2.5 %copy.65 = f32[40,3,128]{2,0,1:T(8,128)S(1)} copy(f32[40,3,128]{1,0,2:T(8,128)} %get-tuple-element.24) | data formatting | bytes 122880 | tf_op jit(solution)/shard_map/slice | solution.py:21
  13.1 3.0 %collective-permute-start = (f32[40,3,128]{2,0,1:T(8,128)S(1)}, f32[40,3,128]{2,0,1:T(8,128)S(1)}, u32[]{:S(2)}, u32[]{:S(2)}) collective-permute-start(f32[40,3,128]{2,0,1:T(8,128)S(1)} %copy.65), channel_id=1, source_target_pairs={{0,4},{4,8},{8,12},{12,16},{16,20},{20,24},{24,28},{1,5},{5,9},{9,... | collective-permute-start | bytes 184328 | tf_op jit(solution)/shard_map/ppermute | solution.py:23
  17.3 2.3 %copy.68 = f32[40,3,128]{1,0,2:T(8,128)} copy(f32[40,3,128]{2,0,1:T(8,128)S(1)} %collective-permute-done.1) | data formatting | bytes 122880 | tf_op jit(solution)/shard_map/ppermute | solution.py:24
  19.6 2.3 %copy.66 = f32[40,3,128]{1,0,2:T(8,128)} copy(f32[40,3,128]{2,0,1:T(8,128)S(1)} %collective-permute-done) | data formatting | bytes 122880 | tf_op jit(solution)/shard_map/ppermute | solution.py:23
  24.5 2.7 %maximum_maximum_fusion.1 = (f32[40,131,128]{1,0,2:T(8,128)S(1)}, f32[40,131,128]{1,0,2:T(8,128)S(1)}) fusion(f32[2,128,128]{1,0,2:T(2,128)S(1)} %copy.64, f32[38,128,128]{1,0,2:T(8,128)S(1)} %copy.75, f32[40,3,128]{1,0,2:T(8,128)S(1)} %copy-done.2, f32[40,3,128]{1,0,2:T(8,128)S(1)} %copy-done.1), kind=kLoop, calls=%fused_computation.3 | loop fusion | flops 2682880 | bytes 8110080 | tf_op jit(solution)/shard_map/concatenate | solution.py:25
  28.0 4.9 %collective-permute-start.2 = (f32[40,134,3]{1,0,2:T(8,128)S(1)}, f32[40,134,3]{1,0,2:T(8,128)S(1)}, u32[]{:S(2)}, u32[]{:S(2)}) collective-permute-start(f32[40,134,3]{1,0,2:T(8,128)S(1)} %get-tuple-element.20), channel_id=1, source_target_pairs={{0,1},{1,2},{2,3},{4,5},{5,6},{6,7},{8,9},{9,10},{10,11},{12,13},{... | collective-permute-start | bytes 192968 | tf_op jit(solution)/shard_map/ppermute | solution.py:23
  34.5 25.3 %multiply_add_fusion = f32[38,129,128]{1,0,2:T(8,128)} fusion(f32[40,131,128]{1,0,2:T(8,128)S(1)} %get-tuple-element.23, f32[40,131,128]{1,0,2:T(8,128)S(1)} %get-tuple-element.22, f32[129,128]{0,1:T(8,128)S(1)} %get-tuple-element.28, f32[129,128]{0,1:T(8,128)S(1)} %get-tuple-element.29), kind=kLoop, calls=%fused_computation.5 | loop fusion | flops 77177088 | bytes 17700864 | tf_op jit(solution)/shard_map/add | solution.py:65
  60.2 7.2 %maximum_maximum_fusion = (f32[40,134,131]{1,0,2:T(8,128)S(1)}, f32[40,134,131]{1,0,2:T(8,128)S(1)}) fusion(f32[40,3,128]{1,0,2:T(8,128)S(1)} %copy-done.1, f32[2,128,128]{1,0,2:T(2,128)S(1)} %copy.64, f32[38,128,128]{1,0,2:T(8,128)S(1)} %copy.75, f32[40,3,128]{1,0,2:T(8,128)S(1)} %copy-done.2, f32[40,134,3]{1,0,2:T(8,128)S(1)} %collective-permute-done.2, ...), kind=kLoop, calls=%fused_computation.1 | loop fusion | flops 5617280 | bytes 8490240 | tf_op jit(solution)/shard_map/concatenate | solution.py:25
  67.4 13.0 %multiply_add_fusion.3 = f32[38,128,129]{1,0,2:T(8,128)S(1)} fusion(f32[40,134,131]{1,0,2:T(8,128)S(1)} %get-tuple-element.19, f32[40,134,131]{1,0,2:T(8,128)S(1)} %get-tuple-element.18, f32[128,129]{0,1:T(8,128)S(1)} %get-tuple-element.26, f32[128,129]{0,1:T(8,128)S(1)} %get-tuple-element.27), kind=kLoop, calls=%fused_computation.31 | loop fusion | flops 77177088 | bytes 17700864 | tf_op jit(solution)/shard_map/add | solution.py:65
  80.5 4.3 %fusion.44 = f32[38,128,128]{1,0,2:T(8,128)S(1)} fusion(f32[38,128,128]{1,0,2:T(8,128)S(1)} %copy.75, f32[38,128,129]{1,0,2:T(8,128)S(1)} %multiply_add_fusion.3, f32[38,129,128]{1,0,2:T(8,128)} %multiply_add_fusion), kind=kLoop, calls=%fused_computation.60 | loop fusion | flops 3112960 | bytes 14942208 | tf_op jit(solution)/shard_map/sub | solution.py:77
  84.8 2.5 %fusion.78 = f32[128,128,38]{0,2,1:T(8,128)S(1)} fusion(f32[38,128,128]{1,0,2:T(8,128)S(1)} %fusion.44, f32[38,38]{1,0:T(8,128)S(1)} %copy-done), kind=kOutput, calls=%fused_computation.113 | convolution fusion | flops 283901952 | bytes 4986512 | tf_op jit(solution)/shard_map/dot_general | solution.py:89
  87.3 4.1 %bitcast_subtract_fusion.4 = f32[38,128,128]{1,0,2:T(8,128)S(1)} fusion(f32[38,128,128]{1,0,2:T(8,128)S(1)} %fusion.44, f32[128,128,38]{0,2,1:T(8,128)S(1)} %fusion.78, f32[128,128]{0,1:T(8,128)S(1)} %copy.76, f32[38,38]{1,0:T(8,128)S(1)} %copy-done.4), kind=kOutput, calls=%fused_computation.73 | convolution fusion | flops 290127872 | bytes 7542416 | tf_op jit(solution)/shard_map/dot_general | solution.py:96
  91.4 2.4 %fusion.76 = f32[128,128,38]{0,2,1:T(8,128)S(1)} fusion(f32[38,128,128]{1,0,2:T(8,128)S(1)} %bitcast_subtract_fusion.4, f32[38,38]{1,0:T(8,128)S(1)} %copy-done), kind=kOutput, calls=%fused_computation.111 | convolution fusion | flops 283901952 | bytes 4986512 | tf_op jit(solution)/shard_map/dot_general | solution.py:89
  93.8 4.5 %bitcast_subtract_fusion.2 = f32[38,128,128]{1,0,2:T(8,128)S(1)} fusion(f32[38,128,128]{1,0,2:T(8,128)S(1)} %bitcast_subtract_fusion.4, f32[128,128,38]{0,2,1:T(8,128)S(1)} %fusion.76, f32[38,128,128]{1,0,2:T(8,128)S(1)} %fusion.44, f32[128,128]{0,1:T(8,128)S(1)} %copy.76, f32[38,38]{1,0:T(8,128)S(1)} %copy-done.4), kind=kOutput, calls=%fused_computation.69 | convolution fusion | flops 290127872 | bytes 10032784 | tf_op jit(solution)/shard_map/dot_general | solution.py:96
  98.3 2.3 %fusion.74 = f32[128,128,38]{0,2,1:T(8,128)S(1)} fusion(f32[38,128,128]{1,0,2:T(8,128)S(1)} %bitcast_subtract_fusion.2, f32[38,38]{1,0:T(8,128)S(1)} %copy-done), kind=kOutput, calls=%fused_computation.109 | convolution fusion | flops 283901952 | bytes 4986512 | tf_op jit(solution)/shard_map/dot_general | solution.py:89
  100.6 4.4 %fusion.45 = f32[38,128,128]{1,0,2:T(8,128)S(1)} fusion(f32[38,128,128]{1,0,2:T(8,128)S(1)} %fusion.44, f32[38,128,128]{1,0,2:T(8,128)S(1)} %bitcast_subtract_fusion.2, f32[128,128,38]{0,2,1:T(8,128)S(1)} %fusion.74, f32[128,128]{0,1:T(8,128)S(1)} %copy.76, pred[128]{0:T(512)(128)(4,1)S(1)} %gt.22, f32[38,38]{1,0:T(8,128)S(1)} %copy-done.4), kind=kOutput, calls=%fused_computation.65 | convolution fusion | flops 290750464 | bytes 10032912 | tf_op jit(solution)/shard_map/dot_general | solution.py:96
  104.9 2.1 %copy.77 = f32[38,128,128]{2,1,0:T(8,128)} copy(f32[38,128,128]{1,0,2:T(8,128)S(1)} %fusion.45) | data formatting | bytes 4980736
  107.1 1.7 %convolution_bitcast_fusion = f32[4,128,128]{1,0,2:T(4,128)S(1)} fusion(f32[38,128,128]{1,0,2:T(8,128)S(1)} %fusion.45, f32[4,38]{1,0:T(4,128)S(1)} %copy-done.7), kind=kOutput, calls=%fused_computation.85 | convolution fusion | flops 29884416 | bytes 2753120 | tf_op jit(solution)/shard_map/dot_general | solution.py:102
  109.1 13.0 %psum.7 = f32[4,128]{1,0:T(4,128)S(1)} all-reduce(f32[4,128]{1,0:T(4,128)S(1)} %broadcast_multiply_fusion), channel_id=1, replica_groups=mesh['axial'=8,'radial'=4] {'radial'}, use_global_device_ids=true, to_apply=%region_0.1 | all-reduce | flops 512 | bytes 4096 | tf_op jit(solution)/shard_map/psum | solution.py:141
  122.1 10.3 %all_gather.3 = f32[4,1024]{1,0:T(4,128)S(1)} all-gather(f32[4,128]{1,0:T(4,128)S(1)} %psum.7), channel_id=1, replica_groups=mesh['axial'=8,'radial'=4] {'axial'}, dimensions={1}, use_global_device_ids=true | all-gather | bytes 18432 | tf_op jit(solution)/shard_map/all_gather | solution.py:142
  132.4 35.0 %gather_fusion = f32[4096]{0:T(1024)S(1)} fusion(f32[4,1024]{1,0:T(4,128)S(1)} %all_gather.3, s32[4096]{0:T(1024)S(1)} %bitcast.92), kind=kCustom, calls=%fused_computation | custom fusion | bytes 65536 | tf_op jit(solution)/shard_map/jit(take_along_axis)/gather | solution.py:148
  (45 shorter events, 9.6 us)
Async XLA Ops:
  0.6 84.1 %copy-start = (f32[38,38]{1,0:T(8,128)S(1)}, f32[38,38]{1,0:T(8,128)}, u32[]{:S(2)}) copy-start(f32[38,38]{1,0:T(8,128)} %param.13) | copy-start | bytes 17332
  0.6 2.6 %copy-start.3 = (f32[2,128,128]{2,1,0:T(8,128)S(1)}, f32[2,128,128]{2,1,0:T(8,128)}, u32[]{:S(2)}) copy-start(f32[2,128,128]{2,1,0:T(8,128)} %param.11) | copy-start | bytes 393220
  6.7 9.4 %copy-start.5 = (f32[128,128]{1,0:T(8,128)S(1)}, f32[128,128]{1,0:T(8,128)}, u32[]{:S(2)}) copy-start(f32[128,128]{1,0:T(8,128)} %param.12) | copy-start | bytes 196612
  6.7 9.6 %copy-start.9 = (s32[64,1]{0,1:T(1,128)S(1)}, s32[64,1]{0,1:T(1,128)}, u32[]{:S(2)}) copy-start(s32[64,1]{0,1:T(1,128)} %param.15) | copy-start | bytes 772
  9.2 8.0 %collective-permute-start.1 = (f32[40,3,128]{2,0,1:T(8,128)S(1)}, f32[40,3,128]{2,0,1:T(8,128)S(1)}, u32[]{:S(2)}, u32[]{:S(2)}) collective-permute-start(f32[40,3,128]{2,0,1:T(8,128)S(1)} %copy.67), channel_id=1, source_target_pairs={{4,0},{8,4},{12,8},{16,12},{20,16},{24,20},{28,24},{5,1},{9,5},{13... | collective-permute-start | bytes 184328 | tf_op jit(solution)/shard_map/ppermute | solution.py:24
  13.1 6.5 %collective-permute-start = (f32[40,3,128]{2,0,1:T(8,128)S(1)}, f32[40,3,128]{2,0,1:T(8,128)S(1)}, u32[]{:S(2)}, u32[]{:S(2)}) collective-permute-start(f32[40,3,128]{2,0,1:T(8,128)S(1)} %copy.65), channel_id=1, source_target_pairs={{0,4},{4,8},{8,12},{12,16},{16,20},{20,24},{24,28},{1,5},{5,9},{9,... | collective-permute-start | bytes 184328 | tf_op jit(solution)/shard_map/ppermute | solution.py:23
  21.9 1.9 %copy-start.1 = (f32[40,3,128]{1,0,2:T(8,128)S(1)}, f32[40,3,128]{1,0,2:T(8,128)}, u32[]{:S(2)}) copy-start(f32[40,3,128]{1,0,2:T(8,128)} %copy.68) | copy-start | bytes 184324
  21.9 2.6 %copy-start.2 = (f32[40,3,128]{1,0,2:T(8,128)S(1)}, f32[40,3,128]{1,0,2:T(8,128)}, u32[]{:S(2)}) copy-start(f32[40,3,128]{1,0,2:T(8,128)} %copy.66) | copy-start | bytes 184324
  28.0 31.9 %collective-permute-start.2 = (f32[40,134,3]{1,0,2:T(8,128)S(1)}, f32[40,134,3]{1,0,2:T(8,128)S(1)}, u32[]{:S(2)}, u32[]{:S(2)}) collective-permute-start(f32[40,134,3]{1,0,2:T(8,128)S(1)} %get-tuple-element.20), channel_id=1, source_target_pairs={{0,1},{1,2},{2,3},{4,5},{5,6},{6,7},{8,9},{9,10},{10,11},{12,13},{... | collective-permute-start | bytes 192968 | tf_op jit(solution)/shard_map/ppermute | solution.py:23
  32.9 26.9 %collective-permute-start.3 = (f32[40,134,3]{1,0,2:T(8,128)S(1)}, f32[40,134,3]{1,0,2:T(8,128)S(1)}, u32[]{:S(2)}, u32[]{:S(2)}) collective-permute-start(f32[40,134,3]{1,0,2:T(8,128)S(1)} %get-tuple-element.21), channel_id=1, source_target_pairs={{1,0},{2,1},{3,2},{5,4},{6,5},{7,6},{9,8},{10,9},{11,10},{13,12},{... | collective-permute-start | bytes 192968 | tf_op jit(solution)/shard_map/ppermute | solution.py:24
  84.8 2.5 %copy-start.4 = (f32[38,38]{1,0:T(8,128)S(1)}, f32[38,38]{1,0:T(8,128)}, u32[]{:S(2)}) copy-start(f32[38,38]{1,0:T(8,128)} %param.14) | copy-start | bytes 17332
  104.9 2.1 %copy-start.7 = (f32[4,38]{1,0:T(4,128)S(1)}, f32[4,38]{1,0:T(4,128)}, u32[]{:S(2)}) copy-start(f32[4,38]{1,0:T(4,128)} %param.16) | copy-start | bytes 1828
  107.1 1.7 %copy-start.8 = (f32[128]{0:T(128)S(1)}, f32[128]{0:T(128)}, u32[]{:S(2)}) copy-start(f32[128]{0:T(128)} %param.17) | copy-start | bytes 1540
  132.4 35.0 %copy-start.6 = (f32[4,1024]{1,0:T(4,128)S(1)}, f32[4,1024]{1,0:T(4,128)}, u32[]{:S(2)}) copy-start(f32[4,1024]{1,0:T(4,128)} %param.19) | copy-start | bytes 49156
where the time goes:
time: 169 us
  other arithmetic  60.4 us (36%)
  local copies, waits for them, and re-layouts  51.3 us (30%)
  blocking collectives  23.3 us (14%)
  matrix products  22.1 us (13%)
  starting transfers between devices  10.7 us (6%)
    add x2, other arithmetic, face_difference(): jnp.maximum(face_speed, 0.0) * left_value  38.3 us
    gather x2, local copies, waits for them, and re-layouts, local(): values = jnp.take_along_axis(whole_profile, own_rows, axis=1)  35 us
    psum x1, blocking collectives, local(): column = lax.psum(profile, 'radial')  13 us
    dot_general x3, matrix products, kinetics_advance(): jnp.tensordot(frozen_jacobian_inverse_addend, defect, axes=(1, 0), precis...  13 us
    all_gather x1, blocking collectives, local(): whole_profile = lax.all_gather(column, 'axial', axis=1, tiled=True)  10.3 us
    concatenate x2, other arithmetic, extended(): shard = jnp.concatenate([before, shard, after], axis=dim)  9.84 us
    ppermute x2, starting transfers between devices, extended(): before = lax.ppermute(last, axis, up)  7.97 us
    dot_general x3, matrix products, kinetics_advance(): jnp.tensordot(linearized_kinetics_operator, current, axes=(1, 0), precisi...  7.12 us
  transfers between devices with their start and end apart: 4, of which 0 were waited for; matrix products, arithmetic and copies ran while one was open for 19% of the time, Pallas kernels for 0%

commit v1 on v0

--- a/solution.py
+++ b/solution.py
@@ -11,6 +11,33 @@
 ARRHENIUS_BARRIER = 1.0
 WENO_EPS = 1e-06
 HIGHEST = lax.Precision.HIGHEST
+
+
+def rest_the_boxes(local_block):
+    r2 = jax.lax.axis_size("axial")
+    carry_out = jax.lax.axis_index("axial")
+    e_now, plain, kept_arr = (r2, carry_out, local_block.shape[1])
+    part_next = map(lambda p: (p, (p + 1) % e_now), range(e_now))
+    all_blocks = list(part_next)
+    front = map(lambda p: (p, (p - 1) % e_now), range(e_now))
+    fields = list(front)
+    base_arr = jnp.zeros(
+        (*local_block.shape[:1], e_now * kept_arr, *local_block.shape[2:]), local_block.dtype
+    )
+    base_arr = lax.dynamic_update_slice_in_dim(base_arr, local_block, plain * kept_arr, axis=1)
+    z = outcome_arr = local_block
+    high = e_now // 2
+    for dev in range(1, high + 1):
+        z = jax.lax.ppermute(z, "axial", all_blocks)
+        base_arr = lax.dynamic_update_slice_in_dim(
+            base_arr, z, (plain - dev) % e_now * kept_arr, axis=1
+        )
+        if dev < e_now - high:
+            outcome_arr = jax.lax.ppermute(outcome_arr, axis_name="axial", perm=fields)
+            base_arr = lax.dynamic_update_slice_in_dim(
+                base_arr, outcome_arr, (plain + dev) % e_now * kept_arr, axis=1
+            )
+    return base_arr
 
 
 def extended(shard, sides, width):
@@ -139,7 +166,7 @@
         * path_scale
     )
     column = lax.psum(profile, "radial")
-    whole_profile = lax.all_gather(column, "axial", axis=1, tiled=True)
+    whole_profile = rest_the_boxes(column)
     device = lax.axis_index(("axial", "radial"))
     sample_count = observed_absorbance_traces.shape[1]
     own_rows = lax.dynamic_slice_in_dim(

time: 169 us -> 175 us (1.036)
  blocking collectives: 23.3 us -> 13 us
  starting transfers between devices: 10.7 us -> 18.6 us
  waiting for transfers between devices: 0.01 us -> 6.44 us
    all_gather x1 -> x0, blocking collectives: 10.3 us -> none  [local(): whole_profile = lax.all_gather(column, 'axial', axis=1, tiled=True)]
    ppermute x0 -> x7, starting transfers between devices: none -> 7.91 us  [the longest x3 7.86 us: rest_the_boxes(): outcome_arr = jax.lax.ppermute(outcome_arr, axis_name='axial', perm=fields)]
    ppermute x0 -> x7, waiting for transfers between devices: none -> 6.43 us  [the longest x4 6.34 us: rest_the_boxes(): z = jax.lax.ppermute(z, 'axial', all_blocks)]
    unnamed x25 -> x27, local copies, waits for them, and re-layouts: 6.29 us -> 7.51 us
  transfers between devices with their start and end apart: 4 -> 11, of which waited for: 0 -> 3; matrix products, arithmetic and copies ran while one was open for 19% -> 20% of each run, Pallas kernels for 0% -> 0%
where the time goes in v1:
time: 175 us
  other arithmetic  60.4 us (35%)
  local copies, waits for them, and re-layouts  52.6 us (30%)
  matrix products  22.3 us (13%)
  starting transfers between devices  18.6 us (11%)
  blocking collectives  13 us (7%)
  waiting for transfers between devices  6.44 us (4%)
    add x2, other arithmetic, face_difference(): jnp.maximum(face_speed, 0.0) * left_value  38.3 us
    gather x2, local copies, waits for them, and re-layouts, local(): values = jnp.take_along_axis(whole_profile, own_rows, axis=1)  35 us
    dot_general x3, matrix products, kinetics_advance(): jnp.tensordot(frozen_jacobian_inverse_addend, defect, axes=(1, 0), precis...  13.1 us
    psum x1, blocking collectives, local(): column = lax.psum(profile, 'radial')  13 us
    concatenate x2, other arithmetic, extended(): shard = jnp.concatenate([before, shard, after], axis=dim)  9.84 us
    ppermute x2, starting transfers between devices, extended(): before = lax.ppermute(last, axis, up)  7.97 us
    ppermute x3, starting transfers between devices, rest_the_boxes(): outcome_arr = jax.lax.ppermute(outcome_arr, axis_name='axial', perm=fields)  7.86 us
    unnamed x27, local copies, waits for them, and re-layouts  7.51 us
  transfers between devices with their start and end apart: 11, of which 3 were waited for; matrix products, arithmetic and copies ran while one was open for 20% of the time, Pallas kernels for 0%

profile of v1, /device:TPU:0, one launch (start us, length us, event | category | flops | bytes accessed | tf_op | source)
XLA Modules:
  0.0 174.6 jit_solution(18335846069664959861)
XLA Ops:
  0.7 2.6 %copy.75 = f32[38,128,128]{1,0,2:T(8,128)S(1)} copy(f32[38,128,128]{2,1,0:T(8,128)} %param.10) | data formatting | bytes 4980736 | tf_op args[0]
  3.4 3.3 %slice_maximum_fusion = (f32[40,3,128]{1,0,2:T(8,128)}, f32[40,3,128]{1,0,2:T(8,128)}) fusion(f32[2,128,128]{1,0,2:T(2,128)S(1)} %copy.64, f32[38,128,128]{1,0,2:T(8,128)S(1)} %copy.75), kind=kLoop, calls=%fused_computation.63 | loop fusion | flops 30720 | bytes 2744320 | tf_op jit(solution)/shard_map/concatenate | solution.py:146
  6.7 2.5 %copy.67 = f32[40,3,128]{2,0,1:T(8,128)S(1)} copy(f32[40,3,128]{1,0,2:T(8,128)} %get-tuple-element.25) | data formatting | bytes 122880 | tf_op jit(solution)/shard_map/slice | solution.py:49
  10.6 2.5 %copy.65 = f32[40,3,128]{2,0,1:T(8,128)S(1)} copy(f32[40,3,128]{1,0,2:T(8,128)} %get-tuple-element.24) | data formatting | bytes 122880 | tf_op jit(solution)/shard_map/slice | solution.py:48
  13.1 3.0 %collective-permute-start = (f32[40,3,128]{2,0,1:T(8,128)S(1)}, f32[40,3,128]{2,0,1:T(8,128)S(1)}, u32[]{:S(2)}, u32[]{:S(2)}) collective-permute-start(f32[40,3,128]{2,0,1:T(8,128)S(1)} %copy.65), channel_id=1, source_target_pairs={{0,4},{4,8},{8,12},{12,16},{16,20},{20,24},{24,28},{1,5},{5,9},{9,... | collective-permute-start | bytes 184328 | tf_op jit(solution)/shard_map/ppermute | solution.py:50
  24.8 2.7 %maximum_maximum_fusion.1 = (f32[40,131,128]{1,0,2:T(8,128)S(1)}, f32[40,131,128]{1,0,2:T(8,128)S(1)}) fusion(f32[2,128,128]{1,0,2:T(2,128)S(1)} %copy.64, f32[38,128,128]{1,0,2:T(8,128)S(1)} %copy.75, f32[40,3,128]{1,0,2:T(8,128)S(1)} %copy-done.2, f32[40,3,128]{1,0,2:T(8,128)S(1)} %copy-done.1), kind=kLoop, calls=%fused_computation.3 | loop fusion | flops 2682880 | bytes 8110080 | tf_op jit(solution)/shard_map/concatenate | solution.py:52
  28.2 4.9 %collective-permute-start.2 = (f32[40,134,3]{1,0,2:T(8,128)S(1)}, f32[40,134,3]{1,0,2:T(8,128)S(1)}, u32[]{:S(2)}, u32[]{:S(2)}) collective-permute-start(f32[40,134,3]{1,0,2:T(8,128)S(1)} %get-tuple-element.20), channel_id=1, source_target_pairs={{0,1},{1,2},{2,3},{4,5},{5,6},{6,7},{8,9},{9,10},{10,11},{12,13},{... | collective-permute-start | bytes 192968 | tf_op jit(solution)/shard_map/ppermute | solution.py:50
  34.8 25.3 %multiply_add_fusion = f32[38,129,128]{1,0,2:T(8,128)} fusion(f32[40,131,128]{1,0,2:T(8,128)S(1)} %get-tuple-element.23, f32[40,131,128]{1,0,2:T(8,128)S(1)} %get-tuple-element.22, f32[129,128]{0,1:T(8,128)S(1)} %get-tuple-element.28, f32[129,128]{0,1:T(8,128)S(1)} %get-tuple-element.29), kind=kLoop, calls=%fused_computation.5 | loop fusion | flops 77177088 | bytes 17700864 | tf_op jit(solution)/shard_map/add | solution.py:92
  60.5 7.2 %maximum_maximum_fusion = (f32[40,134,131]{1,0,2:T(8,128)S(1)}, f32[40,134,131]{1,0,2:T(8,128)S(1)}) fusion(f32[40,3,128]{1,0,2:T(8,128)S(1)} %copy-done.1, f32[2,128,128]{1,0,2:T(2,128)S(1)} %copy.64, f32[38,128,128]{1,0,2:T(8,128)S(1)} %copy.75, f32[40,3,128]{1,0,2:T(8,128)S(1)} %copy-done.2, f32[40,134,3]{1,0,2:T(8,128)S(1)} %collective-permute-done.2, ...), kind=kLoop, calls=%fused_computation.1 | loop fusion | flops 5617280 | bytes 8490240 | tf_op jit(solution)/shard_map/concatenate | solution.py:52
  67.7 13.0 %multiply_add_fusion.3 = f32[38,128,129]{1,0,2:T(8,128)S(1)} fusion(f32[40,134,131]{1,0,2:T(8,128)S(1)} %get-tuple-element.19, f32[40,134,131]{1,0,2:T(8,128)S(1)} %get-tuple-element.18, f32[128,129]{0,1:T(8,128)S(1)} %get-tuple-element.26, f32[128,129]{0,1:T(8,128)S(1)} %get-tuple-element.27), kind=kLoop, calls=%fused_computation.31 | loop fusion | flops 77177088 | bytes 17700864 | tf_op jit(solution)/shard_map/add | solution.py:92
  80.7 4.3 %fusion.44 = f32[38,128,128]{1,0,2:T(8,128)S(1)} fusion(f32[38,128,128]{1,0,2:T(8,128)S(1)} %copy.75, f32[38,128,129]{1,0,2:T(8,128)S(1)} %multiply_add_fusion.3, f32[38,129,128]{1,0,2:T(8,128)} %multiply_add_fusion), kind=kLoop, calls=%fused_computation.60 | loop fusion | flops 3112960 | bytes 14942208 | tf_op jit(solution)/shard_map/sub | solution.py:104
  85.0 2.4 %fusion.78 = f32[128,128,38]{0,2,1:T(8,128)S(1)} fusion(f32[38,128,128]{1,0,2:T(8,128)S(1)} %fusion.44, f32[38,38]{1,0:T(8,128)S(1)} %copy-done), kind=kOutput, calls=%fused_computation.113 | convolution fusion | flops 283901952 | bytes 4986512 | tf_op jit(solution)/shard_map/dot_general | solution.py:116
  87.5 4.1 %bitcast_subtract_fusion.4 = f32[38,128,128]{1,0,2:T(8,128)S(1)} fusion(f32[38,128,128]{1,0,2:T(8,128)S(1)} %fusion.44, f32[128,128,38]{0,2,1:T(8,128)S(1)} %fusion.78, f32[128,128]{0,1:T(8,128)S(1)} %copy.76, f32[38,38]{1,0:T(8,128)S(1)} %copy-done.5), kind=kOutput, calls=%fused_computation.73 | convolution fusion | flops 290127872 | bytes 7542416 | tf_op jit(solution)/shard_map/dot_general | solution.py:123
  91.6 2.5 %fusion.76 = f32[128,128,38]{0,2,1:T(8,128)S(1)} fusion(f32[38,128,128]{1,0,2:T(8,128)S(1)} %bitcast_subtract_fusion.4, f32[38,38]{1,0:T(8,128)S(1)} %copy-done), kind=kOutput, calls=%fused_computation.111 | convolution fusion | flops 283901952 | bytes 4986512 | tf_op jit(solution)/shard_map/dot_general | solution.py:116
  94.1 4.6 %bitcast_subtract_fusion.2 = f32[38,128,128]{1,0,2:T(8,128)S(1)} fusion(f32[38,128,128]{1,0,2:T(8,128)S(1)} %bitcast_subtract_fusion.4, f32[128,128,38]{0,2,1:T(8,128)S(1)} %fusion.76, f32[38,128,128]{1,0,2:T(8,128)S(1)} %fusion.44, f32[128,128]{0,1:T(8,128)S(1)} %copy.76, f32[38,38]{1,0:T(8,128)S(1)} %copy-done.5), kind=kOutput, calls=%fused_computation.69 | convolution fusion | flops 290127872 | bytes 10032784 | tf_op jit(solution)/shard_map/dot_general | solution.py:123
  98.7 2.4 %fusion.74 = f32[128,128,38]{0,2,1:T(8,128)S(1)} fusion(f32[38,128,128]{1,0,2:T(8,128)S(1)} %bitcast_subtract_fusion.2, f32[38,38]{1,0:T(8,128)S(1)} %copy-done), kind=kOutput, calls=%fused_computation.109 | convolution fusion | flops 283901952 | bytes 4986512 | tf_op jit(solution)/shard_map/dot_general | solution.py:116
  101.1 4.4 %fusion.45 = f32[38,128,128]{1,0,2:T(8,128)S(1)} fusion(f32[38,128,128]{1,0,2:T(8,128)S(1)} %fusion.44, f32[38,128,128]{1,0,2:T(8,128)S(1)} %bitcast_subtract_fusion.2, f32[128,128,38]{0,2,1:T(8,128)S(1)} %fusion.74, f32[128,128]{0,1:T(8,128)S(1)} %copy.76, pred[128]{0:T(512)(128)(4,1)S(1)} %gt.22, f32[38,38]{1,0:T(8,128)S(1)} %copy-done.5), kind=kOutput, calls=%fused_computation.65 | convolution fusion | flops 290750464 | bytes 10032912 | tf_op jit(solution)/shard_map/dot_general | solution.py:123
  107.5 13.0 %psum.7 = f32[4,128]{1,0:T(4,128)S(1)} all-reduce(f32[4,128]{1,0:T(4,128)S(1)} %broadcast_multiply_fusion), channel_id=1, replica_groups=mesh['axial'=8,'radial'=4] {'radial'}, use_global_device_ids=true, to_apply=%region_0.1 | all-reduce | flops 512 | bytes 4096 | tf_op jit(solution)/shard_map/psum | solution.py:168
  120.6 2.6 %collective-permute-start.5 = (f32[4,128]{1,0:T(4,128)S(1)}, f32[4,128]{1,0:T(4,128)S(1)}, u32[]{:S(2)}, u32[]{:S(2)}) collective-permute-start(f32[4,128]{1,0:T(4,128)S(1)} %psum.7), channel_id=1, source_target_pairs={{0,28},{4,0},{8,4},{12,8},{16,12},{20,16},{24,20},{28,24},{1,29},{... | collective-permute-start | bytes 6152 | tf_op jit(solution)/shard_map/ppermute | solution.py:36
  123.2 3.3 %copy.77 = f32[38,128,128]{2,1,0:T(8,128)} copy(f32[38,128,128]{1,0,2:T(8,128)} %copy-done.3) | data formatting | bytes 4980736
  126.6 2.6 %collective-permute-start.7 = (f32[4,128]{1,0:T(4,128)S(1)}, f32[4,128]{1,0:T(4,128)S(1)}, u32[]{:S(2)}, u32[]{:S(2)}) collective-permute-start(f32[4,128]{1,0:T(4,128)S(1)} %collective-permute-done.5), channel_id=1, source_target_pairs={{0,28},{4,0},{8,4},{12,8},{16,12},{20,16},{24,20},{28,24},{1,29},{... | collective-permute-start | bytes 6152 | tf_op jit(solution)/shard_map/ppermute | solution.py:36
  130.5 2.6 %collective-permute-start.9 = (f32[4,128]{1,0:T(4,128)S(1)}, f32[4,128]{1,0:T(4,128)S(1)}, u32[]{:S(2)}, u32[]{:S(2)}) collective-permute-start(f32[4,128]{1,0:T(4,128)S(1)} %collective-permute-done.7), channel_id=1, source_target_pairs={{0,28},{4,0},{8,4},{12,8},{16,12},{20,16},{24,20},{28,24},{1,29},{... | collective-permute-start | bytes 6152 | tf_op jit(solution)/shard_map/ppermute | solution.py:36
  134.4 3.9 %collective-permute-done.10 = f32[4,128]{1,0:T(4,128)S(1)} collective-permute-done((f32[4,128]{1,0:T(4,128)S(1)}, f32[4,128]{1,0:T(4,128)S(1)}, u32[]{:S(2)}, u32[]{:S(2)}) %collective-permute-start.10) | collective-permute-done | bytes 2080 | tf_op jit(solution)/shard_map/ppermute | solution.py:31
  138.3 35.0 %gather_fusion = f32[4096]{0:T(1024)S(1)} fusion(f32[4,1024]{1,0:T(4,128)S(1)} %constant_dynamic-update-slice_fusion, s32[4096]{0:T(1024)S(1)} %bitcast.92), kind=kCustom, calls=%fused_computation | custom fusion | bytes 65536 | tf_op jit(solution)/shard_map/jit(take_along_axis)/gather | solution.py:175
  (69 shorter events, 18.6 us)
Async XLA Ops:
  0.6 84.4 %copy-start = (f32[38,38]{1,0:T(8,128)S(1)}, f32[38,38]{1,0:T(8,128)}, u32[]{:S(2)}) copy-start(f32[38,38]{1,0:T(8,128)} %param.13) | copy-start | bytes 17332
  0.6 2.6 %copy-start.4 = (f32[2,128,128]{2,1,0:T(8,128)S(1)}, f32[2,128,128]{2,1,0:T(8,128)}, u32[]{:S(2)}) copy-start(f32[2,128,128]{2,1,0:T(8,128)} %param.11) | copy-start | bytes 393220
  6.7 9.5 %copy-start.6 = (f32[128,128]{1,0:T(8,128)S(1)}, f32[128,128]{1,0:T(8,128)}, u32[]{:S(2)}) copy-start(f32[128,128]{1,0:T(8,128)} %param.12) | copy-start | bytes 196612
  6.7 9.7 %copy-start.10 = (s32[64,1]{0,1:T(1,128)S(1)}, s32[64,1]{0,1:T(1,128)}, u32[]{:S(2)}) copy-start(s32[64,1]{0,1:T(1,128)} %param.15) | copy-start | bytes 772
  9.3 8.2 %collective-permute-start.1 = (f32[40,3,128]{2,0,1:T(8,128)S(1)}, f32[40,3,128]{2,0,1:T(8,128)S(1)}, u32[]{:S(2)}, u32[]{:S(2)}) collective-permute-start(f32[40,3,128]{2,0,1:T(8,128)S(1)} %copy.67), channel_id=1, source_target_pairs={{4,0},{8,4},{12,8},{16,12},{20,16},{24,20},{28,24},{5,1},{9,5},{13... | collective-permute-start | bytes 184328 | tf_op jit(solution)/shard_map/ppermute | solution.py:51
  13.1 6.7 %collective-permute-start = (f32[40,3,128]{2,0,1:T(8,128)S(1)}, f32[40,3,128]{2,0,1:T(8,128)S(1)}, u32[]{:S(2)}, u32[]{:S(2)}) collective-permute-start(f32[40,3,128]{2,0,1:T(8,128)S(1)} %copy.65), channel_id=1, source_target_pairs={{0,4},{4,8},{8,12},{12,16},{16,20},{20,24},{24,28},{1,5},{5,9},{9,... | collective-permute-start | bytes 184328 | tf_op jit(solution)/shard_map/ppermute | solution.py:50
  22.1 1.9 %copy-start.1 = (f32[40,3,128]{1,0,2:T(8,128)S(1)}, f32[40,3,128]{1,0,2:T(8,128)}, u32[]{:S(2)}) copy-start(f32[40,3,128]{1,0,2:T(8,128)} %copy.68) | copy-start | bytes 184324
  22.1 2.6 %copy-start.2 = (f32[40,3,128]{1,0,2:T(8,128)S(1)}, f32[40,3,128]{1,0,2:T(8,128)}, u32[]{:S(2)}) copy-start(f32[40,3,128]{1,0,2:T(8,128)} %copy.66) | copy-start | bytes 184324
  28.2 31.9 %collective-permute-start.2 = (f32[40,134,3]{1,0,2:T(8,128)S(1)}, f32[40,134,3]{1,0,2:T(8,128)S(1)}, u32[]{:S(2)}, u32[]{:S(2)}) collective-permute-start(f32[40,134,3]{1,0,2:T(8,128)S(1)} %get-tuple-element.20), channel_id=1, source_target_pairs={{0,1},{1,2},{2,3},{4,5},{5,6},{6,7},{8,9},{9,10},{10,11},{12,13},{... | collective-permute-start | bytes 192968 | tf_op jit(solution)/shard_map/ppermute | solution.py:50
  33.1 26.9 %collective-permute-start.3 = (f32[40,134,3]{1,0,2:T(8,128)S(1)}, f32[40,134,3]{1,0,2:T(8,128)S(1)}, u32[]{:S(2)}, u32[]{:S(2)}) collective-permute-start(f32[40,134,3]{1,0,2:T(8,128)S(1)} %get-tuple-element.21), channel_id=1, source_target_pairs={{1,0},{2,1},{3,2},{5,4},{6,5},{7,6},{9,8},{10,9},{11,10},{13,12},{... | collective-permute-start | bytes 192968 | tf_op jit(solution)/shard_map/ppermute | solution.py:51
  85.0 2.5 %copy-start.5 = (f32[38,38]{1,0:T(8,128)S(1)}, f32[38,38]{1,0:T(8,128)}, u32[]{:S(2)}) copy-start(f32[38,38]{1,0:T(8,128)} %param.14) | copy-start | bytes 17332
  101.1 4.4 %copy-start.8 = (f32[4,38]{1,0:T(4,128)S(1)}, f32[4,38]{1,0:T(4,128)}, u32[]{:S(2)}) copy-start(f32[4,38]{1,0:T(4,128)} %param.16) | copy-start | bytes 1828
  105.5 15.1 %copy-start.3 = (f32[38,128,128]{1,0,2:T(8,128)}, f32[38,128,128]{1,0,2:T(8,128)S(1)}, u32[]{:S(2)}) copy-start(f32[38,128,128]{1,0,2:T(8,128)S(1)} %fusion.45) | copy-start | bytes 7471108
  105.5 1.7 copy-start.9
  120.5 6.0 %collective-permute-start.4 = (f32[4,128]{1,0:T(4,128)S(1)}, f32[4,128]{1,0:T(4,128)S(1)}, u32[]{:S(2)}, u32[]{:S(2)}) collective-permute-start(f32[4,128]{1,0:T(4,128)S(1)} %psum.7), channel_id=1, source_target_pairs={{0,4},{4,8},{8,12},{12,16},{16,20},{20,24},{24,28},{28,0},{1,5},{5... | collective-permute-start | bytes 6152 | tf_op jit(solution)/shard_map/ppermute | solution.py:31
  120.6 6.0 %collective-permute-start.5 = (f32[4,128]{1,0:T(4,128)S(1)}, f32[4,128]{1,0:T(4,128)S(1)}, u32[]{:S(2)}, u32[]{:S(2)}) collective-permute-start(f32[4,128]{1,0:T(4,128)S(1)} %psum.7), channel_id=1, source_target_pairs={{0,28},{4,0},{8,4},{12,8},{16,12},{20,16},{24,20},{28,24},{1,29},{... | collective-permute-start | bytes 6152 | tf_op jit(solution)/shard_map/ppermute | solution.py:36
  126.5 3.9 %collective-permute-start.6 = (f32[4,128]{1,0:T(4,128)S(1)}, f32[4,128]{1,0:T(4,128)S(1)}, u32[]{:S(2)}, u32[]{:S(2)}) collective-permute-start(f32[4,128]{1,0:T(4,128)S(1)} %collective-permute-done.4), channel_id=1, source_target_pairs={{0,4},{4,8},{8,12},{12,16},{16,20},{20,24},{24,28},{28,0},{1,5},{5... | collective-permute-start | bytes 6152 | tf_op jit(solution)/shard_map/ppermute | solution.py:31
  126.6 4.0 %collective-permute-start.7 = (f32[4,128]{1,0:T(4,128)S(1)}, f32[4,128]{1,0:T(4,128)S(1)}, u32[]{:S(2)}, u32[]{:S(2)}) collective-permute-start(f32[4,128]{1,0:T(4,128)S(1)} %collective-permute-done.5), channel_id=1, source_target_pairs={{0,28},{4,0},{8,4},{12,8},{16,12},{20,16},{24,20},{28,24},{1,29},{... | collective-permute-start | bytes 6152 | tf_op jit(solution)/shard_map/ppermute | solution.py:36
  130.5 3.9 %collective-permute-start.8 = (f32[4,128]{1,0:T(4,128)S(1)}, f32[4,128]{1,0:T(4,128)S(1)}, u32[]{:S(2)}, u32[]{:S(2)}) collective-permute-start(f32[4,128]{1,0:T(4,128)S(1)} %collective-permute-done.6), channel_id=1, source_target_pairs={{0,4},{4,8},{8,12},{12,16},{16,20},{20,24},{24,28},{28,0},{1,5},{5... | collective-permute-start | bytes 6152 | tf_op jit(solution)/shard_map/ppermute | solution.py:31
  130.5 3.9 %collective-permute-start.9 = (f32[4,128]{1,0:T(4,128)S(1)}, f32[4,128]{1,0:T(4,128)S(1)}, u32[]{:S(2)}, u32[]{:S(2)}) collective-permute-start(f32[4,128]{1,0:T(4,128)S(1)} %collective-permute-done.7), channel_id=1, source_target_pairs={{0,28},{4,0},{8,4},{12,8},{16,12},{20,16},{24,20},{28,24},{1,29},{... | collective-permute-start | bytes 6152 | tf_op jit(solution)/shard_map/ppermute | solution.py:36
  134.4 3.9 %collective-permute-start.10 = (f32[4,128]{1,0:T(4,128)S(1)}, f32[4,128]{1,0:T(4,128)S(1)}, u32[]{:S(2)}, u32[]{:S(2)}) collective-permute-start(f32[4,128]{1,0:T(4,128)S(1)} %collective-permute-done.8), channel_id=1, source_target_pairs={{0,4},{4,8},{8,12},{12,16},{16,20},{20,24},{24,28},{28,0},{1,5},{5... | collective-permute-start | bytes 6152 | tf_op jit(solution)/shard_map/ppermute | solution.py:31
  138.3 35.0 %copy-start.7 = (f32[4,1024]{1,0:T(4,128)S(1)}, f32[4,1024]{1,0:T(4,128)}, u32[]{:S(2)}) copy-start(f32[4,1024]{1,0:T(4,128)} %param.19) | copy-start | bytes 49156
